TPU v7x, 768 devices: a whole 4x8x12 slice. The times are simulated.
768 devices in a mesh: face: 96 (over z_lo, y, core), tile: 8 (over x, z_hi).
Axes of the slice: x: 4, y: 8, z: 12 (z_hi: 2, z_lo: 6; z = z_hi * 6 + z_lo), core: 2. Of those that a mesh axis runs over, the one named last changes fastest.
Arguments:
- state: float32 [768, 4, 2, 128, 128], P(('face', 'tile')), may hold values from -3 to 3
- forcing: float32 [768, 2, 4, 128, 128], P(('face', 'tile')), may hold values from -3 to 3
- cotangent: float32 [768, 4, 2, 128, 128], P(('face', 'tile')), may hold values from -6 to 6
- neighbour: int32 [768, 4], P(('face', 'tile')), may hold values from -1 to 767, as said below
- rotation: int32 [768, 4], P(('face', 'tile')), may hold values from 0 to 7
- wet: int32 [768], P(('face', 'tile')), may hold values from 0 to 1, as said below
- levels: int32 [768, 128, 128], P(('face', 'tile')), may hold values from 0 to 2
Outputs:
- state_gradient: float32 [768, 4, 2, 128, 128], P(('face', 'tile'))
- forcing_gradient: float32 [768, 2, 4, 128, 128], P(('face', 'tile'))
Inputs may be any that keep to these rules, and one draw needn't show every extreme that they name: The west neighbour of every tile is the tile of the same slot on the device with the same tile index at face index one below (wrapping around the face axis), the east neighbour the one at face index one above; south and north neighbours lie on a device of the same face block or are -1. Every tile on a device of tile index 0 is wet.
All inputs are finite; a program needn't handle non-finite values.
Results may differ from a plain program's by a relative error of at most 0.00005.
Values sent between devices are 32-bit elements; how exact they have to be, the bound alone decides.
No kernel may reach another device: no remote copies, remote signals or barrier semaphores. Data moves between devices by JAX's collectives and lax.ppermute only.
A program may use at most 32 MiB of HBM per device.

v0:
```python
import jax
import jax.numpy as jnp
from jax import lax
from jax.sharding import PartitionSpec as P

time_step = 1.0
diffuse_rate = 0.15
viscosity = 0.15
vertical_mix = 0.1
coriolis = 0.3
buoyancy_scale = 0.25
thermal_coef = 1.0
haline_coef = 0.8
drag_rate = 0.05


def with_halo(block, sides, width):
    for axis, dim in sides:
        count = lax.axis_size(axis)
        forward = [(i, i + 1) for i in range(count - 1)]
        forward.append((count - 1, 0))
        backward = [(target, source) for source, target in forward]
        low = lax.ppermute(
            lax.slice_in_dim(block, block.shape[dim] - width, None, axis=dim), axis, forward
        )
        high = lax.ppermute(lax.slice_in_dim(block, 0, width, axis=dim), axis, backward)
        block = jnp.concatenate([low, block, high], axis=dim)
    return block


def edge_strips(field):
    return jnp.stack(
        [field[..., :, 0], field[..., :, -1], field[..., 0, :], field[..., -1, :]], axis=1
    )


def place_halo(field, halos):
    padded = jnp.pad(field, ((0, 0), (0, 0), (0, 0), (1, 1), (1, 1)))
    padded = padded.at[..., 1:-1, 0].set(halos[:, 0])
    padded = padded.at[..., 1:-1, -1].set(halos[:, 1])
    padded = padded.at[..., 0, 1:-1].set(halos[:, 2])
    padded = padded.at[..., -1, 1:-1].set(halos[:, 3])
    return padded


def level_mix(values):
    above = jnp.concatenate([values[:, :1], values[:, :-1]], axis=1)
    below = jnp.concatenate([values[:, 1:], values[:, -1:]], axis=1)
    return above + below - 2.0 * values


def step_tiles(padded, mask, drive):
    centre = padded[..., 1:-1, 1:-1]
    east = padded[..., 1:-1, 2:]
    west = padded[..., 1:-1, :-2]
    north = padded[..., 2:, 1:-1]
    south = padded[..., :-2, 1:-1]
    laplace = east + west + north + south - 4.0 * centre
    grad_x = 0.5 * (east - west)
    grad_y = 0.5 * (north - south)
    theta = centre[:, 0]
    salt = centre[:, 1]
    uvel = centre[:, 2]
    vvel = centre[:, 3]
    dens_x = -thermal_coef * grad_x[:, 0] + haline_coef * grad_x[:, 1]
    dens_y = -thermal_coef * grad_y[:, 0] + haline_coef * grad_y[:, 1]
    new_theta = theta + time_step * (
        -(uvel * grad_x[:, 0] + vvel * grad_y[:, 0])
        + diffuse_rate * laplace[:, 0]
        + vertical_mix * level_mix(theta)
    )
    new_salt = salt + time_step * (
        -(uvel * grad_x[:, 1] + vvel * grad_y[:, 1])
        + diffuse_rate * laplace[:, 1]
        + vertical_mix * level_mix(salt)
    )
    new_u = uvel + time_step * (
        viscosity * laplace[:, 2] + coriolis * vvel - buoyancy_scale * dens_x - drag_rate * uvel
    )
    new_v = vvel + time_step * (
        viscosity * laplace[:, 3] - coriolis * uvel - buoyancy_scale * dens_y - drag_rate * vvel
    )
    result = jnp.stack([new_theta, new_salt, new_u, new_v], axis=1)
    result = result.at[:, :, 0].add(time_step * drive)
    return result * mask[:, None]


def shards(state, forcing, cotangent, neighbour, rotation, wet, levels):
    slot_count = state.shape[0]
    group_size = lax.axis_size("tile")
    face_count = lax.axis_size("face")
    face_index = lax.axis_index("face")
    depth = jnp.arange(state.shape[2], dtype=jnp.int32)[None, :, None, None]
    mask = ((depth < levels[:, None]) & (wet[:, None, None, None] == 1)).astype(jnp.float32)
    valid = neighbour >= 0
    source = jnp.maximum(neighbour, 0)
    device_of = source // slot_count
    slot_of = source % slot_count
    source_face = device_of // group_size
    source_tile = device_of % group_size
    side = rotation % 4
    flip = rotation // 4
    lower_face = (face_index + face_count - 1) % face_count
    block = jnp.where(
        source_face == face_index,
        source_tile,
        jnp.where(source_face == lower_face, group_size, group_size + 1),
    )
    column = (block * slot_count + slot_of) * 4 + side
    total = (group_size + 2) * slot_count * 4
    selector = (
        (column[..., None] == jnp.arange(total, dtype=jnp.int32)) & valid[..., None]
    ).astype(jnp.float32)
    selector = selector.reshape(slot_count * 4, total)
    reverse = (flip == 1)[..., None, None, None]

    def gather_rims(field):
        strips = edge_strips(field)[None]
        grouped = lax.all_gather(strips, "tile", axis=0, tiled=True)
        beside_all = with_halo(strips, (("face", 0),), 1)
        return jnp.concatenate([grouped, beside_all[0:1], beside_all[2:3]], axis=0)

    def assemble(field, candidates):
        flat = candidates.reshape(total, -1)
        chosen = jnp.dot(selector, flat, precision=lax.Precision.HIGHEST)
        chosen = chosen.reshape(slot_count, 4, field.shape[1], field.shape[2], field.shape[3])
        flipped = jnp.where(reverse, chosen[..., ::-1], chosen)
        return place_halo(field, flipped)

    def fill(field):
        return assemble(field, gather_rims(field))

    def fill_back(ct_padded, field):
        cand_shape = (group_size + 2, slot_count, 4, field.shape[1], field.shape[2], field.shape[3])
        blank_cands = jnp.zeros(cand_shape, jnp.float32)
        unused, pull_assemble = jax.vjp(assemble, jnp.zeros_like(field), blank_cands)
        ct_field, ct_cands = pull_assemble(ct_padded)
        back_group = lax.psum_scatter(
            ct_cands[:group_size], "tile", scatter_dimension=0, tiled=True
        )
        back_face = with_halo(ct_cands[group_size:], (("face", 0),), 1)
        ct_strips = back_group[0] + back_face[0] + back_face[3]
        unused_edges, pull_edges = jax.vjp(edge_strips, jnp.zeros_like(field))
        (extra,) = pull_edges(ct_strips)
        return ct_field + extra

    def stepper(padded, drive):
        return step_tiles(padded, mask, drive)

    first = state * mask[:, None]
    padded_first = fill(first)
    second = step_tiles(padded_first, mask, forcing[:, 0])
    padded_second = fill(second)
    unused_a, pull_second = jax.vjp(stepper, padded_second, forcing[:, 1])
    ct_pad_second, ct_drive_second = pull_second(cotangent)
    ct_second = fill_back(ct_pad_second, second)
    unused_b, pull_first = jax.vjp(stepper, padded_first, forcing[:, 0])
    ct_pad_first, ct_drive_first = pull_first(ct_second)
    ct_first = fill_back(ct_pad_first, first)
    state_gradient = ct_first * mask[:, None]
    forcing_gradient = jnp.stack([ct_drive_first, ct_drive_second], axis=1)
    return (state_gradient, forcing_gradient)


def solution(mesh):
    placed = (
        P(("face", "tile"), None, None, None, None),
        P(("face", "tile"), None, None, None, None),
        P(("face", "tile"), None, None, None, None),
        P(("face", "tile"), None),
        P(("face", "tile"), None),
        P(("face", "tile")),
        P(("face", "tile"), None, None),
    )
    return jax.shard_map(
        shards,
        mesh=mesh,
        in_specs=placed,
        out_specs=(
            P(("face", "tile"), None, None, None, None),
            P(("face", "tile"), None, None, None, None),
        ),
        check_vma=False,
    )
```

profile of v0, /device:TPU:8, one launch (start us, length us, event | category | flops | bytes accessed | tf_op | source)
XLA Modules:
  0.0 477.9 jit_solution(17691799544904209550)
XLA Ops:
  10.4 1.9 collective-permute-start
  12.4 3.6 collective-permute-start.1
  20.0 58.5 %all-gather = f32[8,4,4,2,128]{4,2,3,1,0:T(4,128)S(1)} all-gather(f32[1,4,4,2,128]{4,2,3,1,0:T(4,128)S(1)} %copy.708), channel_id=2, replica_groups=mesh['face'=96,'tile'=8] {'tile'}, dimensions={0}, use_global_device_ids=true | all-gather | bytes 147456 | tf_op jit(solution)/shard_map/all_gather | solution.py:119
  82.3 1.6 scatter.40
  83.8 3.1 scatter.41
  86.9 2.7 scatter.44
  89.6 1.4 scatter.45
  94.4 1.9 collective-permute-start.2
  96.3 3.6 collective-permute-start.3
  100.0 53.9 %all-gather.1 = f32[8,4,4,2,128]{4,2,3,1,0:T(4,128)S(1)} all-gather(f32[1,4,4,2,128]{4,2,3,1,0:T(4,128)S(1)} %copy.722), channel_id=3, replica_groups=mesh['face'=96,'tile'=8] {'tile'}, dimensions={0}, use_global_device_ids=true | all-gather | bytes 147456 | tf_op jit(solution)/shard_map/all_gather | solution.py:119
  157.0 1.5 scatter.46
  158.5 4.1 scatter.49
  162.6 2.7 scatter.50
  165.3 1.4 scatter.51
  173.1 2.0 scatter.55
  178.1 1.9 collective-permute-start.4
  180.0 5.7 %collective-permute-start.5 = (f32[1,1,4,4,2,128]{5,4,3,2,1,0:T(2,128)S(1)}, f32[1,1,4,4,2,128]{5,4,3,2,1,0:T(2,128)S(1)}, u32[]{:S(2)}, u32[]{:S(2)}) collective-permute-start(f32[1,1,4,4,2,128]{5,4,3,2,1,0:T(2,128)S(1)} %slice.859), channel_id=1, source_target_pairs={{8,0},{16,8},{24,16},{32,24},{40,32},{48,40},{56,48},{64,56},{72,6... | collective-permute-start | bytes 49160 | tf_op jit(solution)/shard_map/ppermute | solution.py:26
  185.8 138.1 %all-reduce.77.cloned.1.call-done = f32[8,1,4,4,2,128]{5,3,4,2,1,0:T(4,128)} async-done(((f32[8,1,4,4,2,128]{5,3,4,2,1,0:T(4,128)}), f32[8,1,4,4,2,128]{5,3,4,2,1,0:T(4,128)}) %all-reduce.77.cloned.1.call-update) | async-done | bytes 131088
  326.7 2.2 fusion.2
  333.1 1.4 scatter.56
  334.6 2.7 scatter.59
  339.5 1.9 collective-permute-start.6
  341.4 3.6 collective-permute-start.7
  346.0 122.0 %all-reduce.79.cloned.1.call-done = f32[8,1,4,4,2,128]{5,3,4,2,1,0:T(4,128)} async-done(((f32[8,1,4,4,2,128]{5,3,4,2,1,0:T(4,128)}), f32[8,1,4,4,2,128]{5,3,4,2,1,0:T(4,128)}) %all-reduce.79.cloned.1.call-update) | async-done | bytes 131088
  (194 shorter events, 38.6 us)
Async XLA Ops:
  7.2 316.7 %all-reduce.77.cloned.1.call-start = ((), (), s32[]{:S(2)}) async-start(), calls=%async_computation | async-start | bytes 262144
  9.8 6.3 %copy-start.10 = (f32[1,4,2,128,128]{4,3,2,1,0:T(8,128)S(1)}, f32[1,4,2,128,128]{4,3,2,1,0:T(8,128)}, u32[]{:S(2)}) copy-start(f32[1,4,2,128,128]{4,3,2,1,0:T(8,128)} %param.43) | copy-start | bytes 1572868
  10.4 70.5 %collective-permute-start = (f32[1,1,4,4,2,128]{5,4,3,2,1,0:T(2,128)S(1)}, f32[1,1,4,4,2,128]{5,4,3,2,1,0:T(2,128)S(1)}, u32[]{:S(2)}, u32[]{:S(2)}) collective-permute-start(f32[1,1,4,4,2,128]{5,4,3,2,1,0:T(2,128)S(1)} %fusion.86), channel_id=1, source_target_pairs={{0,8},{8,16},{16,24},{24,32},{32,40},{40,48},{48,56},{56,64},{64,7... | collective-permute-start | bytes 49160 | tf_op jit(solution)/shard_map/ppermute | solution.py:23
  12.4 68.6 %collective-permute-start.1 = (f32[1,1,4,4,2,128]{5,4,3,2,1,0:T(2,128)S(1)}, f32[1,1,4,4,2,128]{5,4,3,2,1,0:T(2,128)S(1)}, u32[]{:S(2)}, u32[]{:S(2)}) collective-permute-start(f32[1,1,4,4,2,128]{5,4,3,2,1,0:T(2,128)S(1)} %fusion.86), channel_id=1, source_target_pairs={{8,0},{16,8},{24,16},{32,24},{40,32},{48,40},{56,48},{64,56},{72,6... | collective-permute-start | bytes 49160 | tf_op jit(solution)/shard_map/ppermute | solution.py:26
  16.1 2.3 copy-start.19
  16.1 2.3 copy-start.20
  16.5 2.7 copy-start.17
  17.6 2.4 copy-start.4
  19.1 135.6 %copy-start.15 = (pred[1,4,1,1,1,1,40]{6,1,5,4,3,2,0:T(4,128)(4,1)}, pred[1,4,1,1,1,1,40]{6,1,5,4,3,2,0:T(4,128)(4,1)S(1)}, u32[]{:S(2)}) copy-start(pred[1,4,1,1,1,1,40]{6,1,5,4,3,2,0:T(4,128)(4,1)S(1)} %fusion.56) | copy-start | bytes 484
  92.6 1.0 copy-start.13
  94.4 59.8 %collective-permute-start.2 = (f32[1,1,4,4,2,128]{5,4,3,2,1,0:T(2,128)S(1)}, f32[1,1,4,4,2,128]{5,4,3,2,1,0:T(2,128)S(1)}, u32[]{:S(2)}, u32[]{:S(2)}) collective-permute-start(f32[1,1,4,4,2,128]{5,4,3,2,1,0:T(2,128)S(1)} %fusion.85), channel_id=1, source_target_pairs={{0,8},{8,16},{16,24},{24,32},{32,40},{40,48},{48,56},{56,64},{64,7... | collective-permute-start | bytes 49160 | tf_op jit(solution)/shard_map/ppermute | solution.py:23
  96.3 57.9 %collective-permute-start.3 = (f32[1,1,4,4,2,128]{5,4,3,2,1,0:T(2,128)S(1)}, f32[1,1,4,4,2,128]{5,4,3,2,1,0:T(2,128)S(1)}, u32[]{:S(2)}, u32[]{:S(2)}) collective-permute-start(f32[1,1,4,4,2,128]{5,4,3,2,1,0:T(2,128)S(1)} %fusion.85), channel_id=1, source_target_pairs={{8,0},{16,8},{24,16},{32,24},{40,32},{48,40},{56,48},{64,56},{72,6... | collective-permute-start | bytes 49160 | tf_op jit(solution)/shard_map/ppermute | solution.py:26
  157.0 5.6 %copy-start.14 = (f32[1,1,4,2,128]{4,3,2,1,0:T(2,128)S(1)}, f32[1,1,4,2,128]{4,3,2,1,0:T(2,128)}, u32[]{:S(2)}) copy-start(f32[1,1,4,2,128]{4,3,2,1,0:T(2,128)} %get-tuple-element.333) | copy-start | bytes 12292
  166.7 1.0 copy-start.8
  175.8 1.0 copy-start.16
  177.1 149.6 %copy-start.9 = (f32[2,128,128]{2,0,1:T(2,128)S(1)}, f32[2,128,128]{2,0,1:T(2,128)}, u32[]{:S(2)}) copy-start(f32[2,128,128]{2,0,1:T(2,128)} %copy.868) | copy-start | bytes 393220
  178.0 290.1 %all-reduce.79.cloned.1.call-start = ((), (), s32[]{:S(2)}) async-start(), calls=%async_computation.1 | async-start | bytes 262144
  178.1 147.2 %collective-permute-start.4 = (f32[1,1,4,4,2,128]{5,4,3,2,1,0:T(2,128)S(1)}, f32[1,1,4,4,2,128]{5,4,3,2,1,0:T(2,128)S(1)}, u32[]{:S(2)}, u32[]{:S(2)}) collective-permute-start(f32[1,1,4,4,2,128]{5,4,3,2,1,0:T(2,128)S(1)} %slice.857), channel_id=1, source_target_pairs={{0,8},{8,16},{16,24},{24,32},{32,40},{40,48},{48,56},{56,64},{64,7... | collective-permute-start | bytes 49160 | tf_op jit(solution)/shard_map/ppermute | solution.py:23
  180.0 145.2 %collective-permute-start.5 = (f32[1,1,4,4,2,128]{5,4,3,2,1,0:T(2,128)S(1)}, f32[1,1,4,4,2,128]{5,4,3,2,1,0:T(2,128)S(1)}, u32[]{:S(2)}, u32[]{:S(2)}) collective-permute-start(f32[1,1,4,4,2,128]{5,4,3,2,1,0:T(2,128)S(1)} %slice.859), channel_id=1, source_target_pairs={{8,0},{16,8},{24,16},{32,24},{40,32},{48,40},{56,48},{64,56},{72,6... | collective-permute-start | bytes 49160 | tf_op jit(solution)/shard_map/ppermute | solution.py:26
  328.9 1.0 copy-start.1
  328.9 1.2 copy-start.3
  337.8 7.3 %copy-start.6 = (f32[1,1,4,128,128]{4,2,3,1,0:T(4,128)S(1)}, f32[1,1,4,128,128]{4,2,3,1,0:T(4,128)}, u32[]{:S(2)}) copy-start(f32[1,1,4,128,128]{4,2,3,1,0:T(4,128)} %slice_bitcast_fusion) | copy-start | bytes 786436
  339.5 129.9 %collective-permute-start.6 = (f32[1,1,4,4,2,128]{5,4,3,2,1,0:T(2,128)S(1)}, f32[1,1,4,4,2,128]{5,4,3,2,1,0:T(2,128)S(1)}, u32[]{:S(2)}, u32[]{:S(2)}) collective-permute-start(f32[1,1,4,4,2,128]{5,4,3,2,1,0:T(2,128)S(1)} %slice.863), channel_id=1, source_target_pairs={{0,8},{8,16},{16,24},{24,32},{32,40},{40,48},{48,56},{56,64},{64,7... | collective-permute-start | bytes 49160 | tf_op jit(solution)/shard_map/ppermute | solution.py:23
  341.4 128.0 %collective-permute-start.7 = (f32[1,1,4,4,2,128]{5,4,3,2,1,0:T(2,128)S(1)}, f32[1,1,4,4,2,128]{5,4,3,2,1,0:T(2,128)S(1)}, u32[]{:S(2)}, u32[]{:S(2)}) collective-permute-start(f32[1,1,4,4,2,128]{5,4,3,2,1,0:T(2,128)S(1)} %slice.865), channel_id=1, source_target_pairs={{8,0},{16,8},{24,16},{32,24},{40,32},{48,40},{56,48},{64,56},{72,6... | collective-permute-start | bytes 49160 | tf_op jit(solution)/shard_map/ppermute | solution.py:26
  (7 other events, 6.3 us)
Sparse Core Ops, SparseCore 0:
  178.1 145.7 all-reduce.76
  339.4 128.6 all-reduce.78
where the time goes:
time: 479 us; the launch traced here: 478 us
  waiting for transfers between devices  260 us (54%)
  blocking collectives  112 us (23%)
  local copies, waits for them, and re-layouts  48.8 us (10%)
  starting transfers between devices  24.4 us (5%)
  between operations  15.8 us (3%)
  other arithmetic  15.4 us (3%)
    unnamed x4, waiting for transfers between devices  260 us
    all_gather x2, blocking collectives, gather_rims(): grouped = lax.all_gather(strips, 'tile', axis=0, tiled=True)  112 us
    ppermute x4, starting transfers between devices, with_halo(): lax.ppermute(lax.slice_in_dim(block, 0, width, axis=dim), axis, backward)  16.7 us
    scatter x4, local copies, waits for them, and re-layouts, place_halo(): padded = padded.at[..., 0, 1:-1].set(halos[:, 2])  9.97 us
    unnamed x53, local copies, waits for them, and re-layouts  9.65 us
  transfers between devices with their start and end apart: 10, of which 2 were waited for; matrix products, arithmetic and copies ran while one was open for 2% of the time, Pallas kernels for 0%

commit v1 on v0

--- a/solution.py
+++ b/solution.py
@@ -101,9 +101,10 @@
     side = rotation % 4
     flip = rotation // 4
     lower_face = (face_index + face_count - 1) % face_count
+    tile_index = lax.axis_index("tile")
     block = jnp.where(
         source_face == face_index,
-        source_tile,
+        (tile_index - source_tile) % group_size,
         jnp.where(source_face == lower_face, group_size, group_size + 1),
     )
     column = (block * slot_count + slot_of) * 4 + side
@@ -114,11 +115,15 @@
     selector = selector.reshape(slot_count * 4, total)
     reverse = (flip == 1)[..., None, None, None]
 
+    def shift_tile(x, k):
+        pairs = [(i, (i + k) % group_size) for i in range(group_size)]
+        return lax.ppermute(x, "tile", pairs)
+
     def gather_rims(field):
         strips = edge_strips(field)[None]
-        grouped = lax.all_gather(strips, "tile", axis=0, tiled=True)
+        grouped = [strips] + [shift_tile(strips, k) for k in range(1, group_size)]
         beside_all = with_halo(strips, (("face", 0),), 1)
-        return jnp.concatenate([grouped, beside_all[0:1], beside_all[2:3]], axis=0)
+        return jnp.concatenate(grouped + [beside_all[0:1], beside_all[2:3]], axis=0)
 
     def assemble(field, candidates):
         flat = candidates.reshape(total, -1)
@@ -135,9 +140,9 @@
         blank_cands = jnp.zeros(cand_shape, jnp.float32)
         unused, pull_assemble = jax.vjp(assemble, jnp.zeros_like(field), blank_cands)
         ct_field, ct_cands = pull_assemble(ct_padded)
-        back_group = lax.psum_scatter(
-            ct_cands[:group_size], "tile", scatter_dimension=0, tiled=True
-        )
+        back_group = ct_cands[0:1]
+        for k in range(1, group_size):
+            back_group = back_group + shift_tile(ct_cands[k : k + 1], -k)
         back_face = with_halo(ct_cands[group_size:], (("face", 0),), 1)
         ct_strips = back_group[0] + back_face[0] + back_face[3]
         unused_edges, pull_edges = jax.vjp(edge_strips, jnp.zeros_like(field))

time: 479 us -> 279 us (0.58)
  the two profiles are of different devices: /device:TPU:8 before, /device:TPU:2 now
where the time goes in v1:
time: 279 us; the launch traced here: 278 us
  starting transfers between devices  204 us (73%)
  local copies, waits for them, and re-layouts  50.5 us (18%)
  other arithmetic  16.1 us (6%)
  waiting for transfers between devices  2.84 us (1%)
    ppermute x28, starting transfers between devices, shift_tile(): return lax.ppermute(x, 'tile', pairs)  154 us
    ppermute x4, starting transfers between devices, with_halo(): lax.ppermute(lax.slice_in_dim(block, 0, width, axis=dim), axis, backward)  42.6 us
    unnamed x62, local copies, waits for them, and re-layouts  9.98 us
    scatter x4, local copies, waits for them, and re-layouts, place_halo(): padded = padded.at[..., 0, 1:-1].set(halos[:, 2])  9.7 us
    ppermute x4, starting transfers between devices, with_halo(): lax.ppermute(lax.slice_in_dim(block, block.shape[dim] - width, None, axis...  7.67 us
    scatter x2, local copies, waits for them, and re-layouts, place_halo(): padded = padded.at[..., 1:-1, -1].set(halos[:, 1])  7.21 us
  transfers between devices with their start and end apart: 36, of which 3 were waited for; matrix products, arithmetic and copies ran while one was open for 4% of the time, Pallas kernels for 0%

profile of v1, /device:TPU:2, one launch (start us, length us, event | category | flops | bytes accessed | tf_op | source)
XLA Modules:
  0.0 277.5 jit_solution(14003362436863813704)
XLA Ops:
  3.9 15.1 %collective-permute-start = (f32[1,1,4,4,2,128]{5,4,3,2,1,0:T(2,128)S(1)}, f32[1,1,4,4,2,128]{5,4,3,2,1,0:T(2,128)S(1)}, u32[]{:S(2)}, u32[]{:S(2)}) collective-permute-start(f32[1,1,4,4,2,128]{5,4,3,2,1,0:T(2,128)S(1)} %maximum_bitcast_fusion), channel_id=1, source_target_pairs={{0,1},{1,2},{2,3},{3,4},{4,5},{5,6},{6,7},{7,0},{8,9},{9,10},{10,1... | collective-permute-start | bytes 49160 | tf_op jit(solution)/shard_map/ppermute | solution.py:120
  22.4 6.5 %collective-permute-start.2 = (f32[1,1,4,4,2,128]{5,4,3,2,1,0:T(2,128)S(1)}, f32[1,1,4,4,2,128]{5,4,3,2,1,0:T(2,128)S(1)}, u32[]{:S(2)}, u32[]{:S(2)}) collective-permute-start(f32[1,1,4,4,2,128]{5,4,3,2,1,0:T(2,128)S(1)} %maximum_bitcast_fusion), channel_id=1, source_target_pairs={{0,3},{1,4},{2,5},{3,6},{4,7},{5,0},{6,1},{7,2},{8,11},{9,12},{10,... | collective-permute-start | bytes 49160 | tf_op jit(solution)/shard_map/ppermute | solution.py:120
  30.9 9.1 %collective-permute-start.4 = (f32[1,1,4,4,2,128]{5,4,3,2,1,0:T(2,128)S(1)}, f32[1,1,4,4,2,128]{5,4,3,2,1,0:T(2,128)S(1)}, u32[]{:S(2)}, u32[]{:S(2)}) collective-permute-start(f32[1,1,4,4,2,128]{5,4,3,2,1,0:T(2,128)S(1)} %maximum_bitcast_fusion), channel_id=1, source_target_pairs={{0,5},{1,6},{2,7},{3,0},{4,1},{5,2},{6,3},{7,4},{8,13},{9,14},{10,... | collective-permute-start | bytes 49160 | tf_op jit(solution)/shard_map/ppermute | solution.py:120
  47.7 4.5 %collective-permute-start.6 = (f32[1,1,4,4,2,128]{5,4,3,2,1,0:T(2,128)S(1)}, f32[1,1,4,4,2,128]{5,4,3,2,1,0:T(2,128)S(1)}, u32[]{:S(2)}, u32[]{:S(2)}) collective-permute-start(f32[1,1,4,4,2,128]{5,4,3,2,1,0:T(2,128)S(1)} %maximum_bitcast_fusion), channel_id=1, source_target_pairs={{0,7},{1,0},{2,1},{3,2},{4,3},{5,4},{6,5},{7,6},{8,15},{9,8},{10,9... | collective-permute-start | bytes 49160 | tf_op jit(solution)/shard_map/ppermute | solution.py:120
  54.1 10.6 %collective-permute-start.8 = (f32[1,1,4,4,2,128]{5,4,3,2,1,0:T(2,128)S(1)}, f32[1,1,4,4,2,128]{5,4,3,2,1,0:T(2,128)S(1)}, u32[]{:S(2)}, u32[]{:S(2)}) collective-permute-start(f32[1,1,4,4,2,128]{5,4,3,2,1,0:T(2,128)S(1)} %maximum_bitcast_fusion), channel_id=1, source_target_pairs={{8,0},{16,8},{24,16},{32,24},{40,32},{48,40},{56,48},{64,56},{72,6... | collective-permute-start | bytes 49160 | tf_op jit(solution)/shard_map/ppermute | solution.py:26
  79.3 7.7 %collective-permute-start.9 = (f32[1,1,4,4,2,128]{5,4,3,2,1,0:T(2,128)S(1)}, f32[1,1,4,4,2,128]{5,4,3,2,1,0:T(2,128)S(1)}, u32[]{:S(2)}, u32[]{:S(2)}) collective-permute-start(f32[1,1,4,4,2,128]{5,4,3,2,1,0:T(2,128)S(1)} %maximum_bitcast_fusion.1), channel_id=1, source_target_pairs={{0,1},{1,2},{2,3},{3,4},{4,5},{5,6},{6,7},{7,0},{8,9},{9,10},{10,1... | collective-permute-start | bytes 49160 | tf_op jit(solution)/shard_map/ppermute | solution.py:120
  89.6 5.9 %collective-permute-start.11 = (f32[1,1,4,4,2,128]{5,4,3,2,1,0:T(2,128)S(1)}, f32[1,1,4,4,2,128]{5,4,3,2,1,0:T(2,128)S(1)}, u32[]{:S(2)}, u32[]{:S(2)}) collective-permute-start(f32[1,1,4,4,2,128]{5,4,3,2,1,0:T(2,128)S(1)} %maximum_bitcast_fusion.1), channel_id=1, source_target_pairs={{0,3},{1,4},{2,5},{3,6},{4,7},{5,0},{6,1},{7,2},{8,11},{9,12},{10,... | collective-permute-start | bytes 49160 | tf_op jit(solution)/shard_map/ppermute | solution.py:120
  95.5 5.4 %collective-permute-start.12 = (f32[1,1,4,4,2,128]{5,4,3,2,1,0:T(2,128)S(1)}, f32[1,1,4,4,2,128]{5,4,3,2,1,0:T(2,128)S(1)}, u32[]{:S(2)}, u32[]{:S(2)}) collective-permute-start(f32[1,1,4,4,2,128]{5,4,3,2,1,0:T(2,128)S(1)} %maximum_bitcast_fusion.1), channel_id=1, source_target_pairs={{0,4},{1,5},{2,6},{3,7},{4,0},{5,1},{6,2},{7,3},{8,12},{9,13},{10,... | collective-permute-start | bytes 49160 | tf_op jit(solution)/shard_map/ppermute | solution.py:120
  100.9 8.6 %collective-permute-start.13 = (f32[1,1,4,4,2,128]{5,4,3,2,1,0:T(2,128)S(1)}, f32[1,1,4,4,2,128]{5,4,3,2,1,0:T(2,128)S(1)}, u32[]{:S(2)}, u32[]{:S(2)}) collective-permute-start(f32[1,1,4,4,2,128]{5,4,3,2,1,0:T(2,128)S(1)} %maximum_bitcast_fusion.1), channel_id=1, source_target_pairs={{0,5},{1,6},{2,7},{3,0},{4,1},{5,2},{6,3},{7,4},{8,13},{9,14},{10,... | collective-permute-start | bytes 49160 | tf_op jit(solution)/shard_map/ppermute | solution.py:120
  112.4 4.4 %collective-permute-start.15 = (f32[1,1,4,4,2,128]{5,4,3,2,1,0:T(2,128)S(1)}, f32[1,1,4,4,2,128]{5,4,3,2,1,0:T(2,128)S(1)}, u32[]{:S(2)}, u32[]{:S(2)}) collective-permute-start(f32[1,1,4,4,2,128]{5,4,3,2,1,0:T(2,128)S(1)} %maximum_bitcast_fusion.1), channel_id=1, source_target_pairs={{0,7},{1,0},{2,1},{3,2},{4,3},{5,4},{6,5},{7,6},{8,15},{9,8},{10,9... | collective-permute-start | bytes 49160 | tf_op jit(solution)/shard_map/ppermute | solution.py:120
  120.0 10.7 %collective-permute-start.17 = (f32[1,1,4,4,2,128]{5,4,3,2,1,0:T(2,128)S(1)}, f32[1,1,4,4,2,128]{5,4,3,2,1,0:T(2,128)S(1)}, u32[]{:S(2)}, u32[]{:S(2)}) collective-permute-start(f32[1,1,4,4,2,128]{5,4,3,2,1,0:T(2,128)S(1)} %maximum_bitcast_fusion.1), channel_id=1, source_target_pairs={{8,0},{16,8},{24,16},{32,24},{40,32},{48,40},{56,48},{64,56},{72,6... | collective-permute-start | bytes 49160 | tf_op jit(solution)/shard_map/ppermute | solution.py:26
  139.4 4.1 %scatter.49 = f32[1,4,2,130,130]{4,3,2,1,0:T(8,128)S(1)} dynamic-update-slice(f32[1,4,2,130,130]{4,3,2,1,0:T(8,128)S(1)} %scatter.46, f32[1,4,2,128,1]{4,3,2,1,0:T(8,128)} %copy.471, s32[]{:T(128)} %constant.518.clone.1, s32[]{:T(128)} %constant.518.clone.1, s32[]{:T(128)} %constant.518.clone.1, s32[]{:T(128)} %constant.517.clone.1, s32[]{:T(128)} %constant.531.clone.1) | dynamic-update-slice | bytes 8196 | tf_op jit(solution)/shard_map/scatter | solution.py:40
  159.6 8.4 %collective-permute-start.18 = (f32[1,1,4,4,2,128]{5,4,3,2,1,0:T(2,128)S(1)}, f32[1,1,4,4,2,128]{5,4,3,2,1,0:T(2,128)S(1)}, u32[]{:S(2)}, u32[]{:S(2)}) collective-permute-start(f32[1,1,4,4,2,128]{5,4,3,2,1,0:T(2,128)S(1)} %slice.941), channel_id=1, source_target_pairs={{0,7},{1,0},{2,1},{3,2},{4,3},{5,4},{6,5},{7,6},{8,15},{9,8},{10,9... | collective-permute-start | bytes 49160 | tf_op jit(solution)/shard_map/ppermute | solution.py:120
  171.3 4.5 %collective-permute-start.20 = (f32[1,1,4,4,2,128]{5,4,3,2,1,0:T(2,128)S(1)}, f32[1,1,4,4,2,128]{5,4,3,2,1,0:T(2,128)S(1)}, u32[]{:S(2)}, u32[]{:S(2)}) collective-permute-start(f32[1,1,4,4,2,128]{5,4,3,2,1,0:T(2,128)S(1)} %slice.945), channel_id=1, source_target_pairs={{0,5},{1,6},{2,7},{3,0},{4,1},{5,2},{6,3},{7,4},{8,13},{9,14},{10,... | collective-permute-start | bytes 49160 | tf_op jit(solution)/shard_map/ppermute | solution.py:120
  175.8 5.4 %collective-permute-start.21 = (f32[1,1,4,4,2,128]{5,4,3,2,1,0:T(2,128)S(1)}, f32[1,1,4,4,2,128]{5,4,3,2,1,0:T(2,128)S(1)}, u32[]{:S(2)}, u32[]{:S(2)}) collective-permute-start(f32[1,1,4,4,2,128]{5,4,3,2,1,0:T(2,128)S(1)} %slice.947), channel_id=1, source_target_pairs={{0,4},{1,5},{2,6},{3,7},{4,0},{5,1},{6,2},{7,3},{8,12},{9,13},{10,... | collective-permute-start | bytes 49160 | tf_op jit(solution)/shard_map/ppermute | solution.py:120
  181.3 6.6 %collective-permute-start.22 = (f32[1,1,4,4,2,128]{5,4,3,2,1,0:T(2,128)S(1)}, f32[1,1,4,4,2,128]{5,4,3,2,1,0:T(2,128)S(1)}, u32[]{:S(2)}, u32[]{:S(2)}) collective-permute-start(f32[1,1,4,4,2,128]{5,4,3,2,1,0:T(2,128)S(1)} %slice.949), channel_id=1, source_target_pairs={{0,3},{1,4},{2,5},{3,6},{4,7},{5,0},{6,1},{7,2},{8,11},{9,12},{10,... | collective-permute-start | bytes 49160 | tf_op jit(solution)/shard_map/ppermute | solution.py:120
  188.0 4.5 %collective-permute-start.23 = (f32[1,1,4,4,2,128]{5,4,3,2,1,0:T(2,128)S(1)}, f32[1,1,4,4,2,128]{5,4,3,2,1,0:T(2,128)S(1)}, u32[]{:S(2)}, u32[]{:S(2)}) collective-permute-start(f32[1,1,4,4,2,128]{5,4,3,2,1,0:T(2,128)S(1)} %slice.951), channel_id=1, source_target_pairs={{0,2},{1,3},{2,4},{3,5},{4,6},{5,7},{6,0},{7,1},{8,10},{9,11},{10,... | collective-permute-start | bytes 49160 | tf_op jit(solution)/shard_map/ppermute | solution.py:120
  192.5 4.5 %collective-permute-start.24 = (f32[1,1,4,4,2,128]{5,4,3,2,1,0:T(2,128)S(1)}, f32[1,1,4,4,2,128]{5,4,3,2,1,0:T(2,128)S(1)}, u32[]{:S(2)}, u32[]{:S(2)}) collective-permute-start(f32[1,1,4,4,2,128]{5,4,3,2,1,0:T(2,128)S(1)} %slice.953), channel_id=1, source_target_pairs={{0,1},{1,2},{2,3},{3,4},{4,5},{5,6},{6,7},{7,0},{8,9},{9,10},{10,1... | collective-permute-start | bytes 49160 | tf_op jit(solution)/shard_map/ppermute | solution.py:120
  199.0 10.8 %collective-permute-start.26 = (f32[1,1,4,4,2,128]{5,4,3,2,1,0:T(2,128)S(1)}, f32[1,1,4,4,2,128]{5,4,3,2,1,0:T(2,128)S(1)}, u32[]{:S(2)}, u32[]{:S(2)}) collective-permute-start(f32[1,1,4,4,2,128]{5,4,3,2,1,0:T(2,128)S(1)} %slice.957), channel_id=1, source_target_pairs={{8,0},{16,8},{24,16},{32,24},{40,32},{48,40},{56,48},{64,56},{72,6... | collective-permute-start | bytes 49160 | tf_op jit(solution)/shard_map/ppermute | solution.py:26
  224.9 8.6 %collective-permute-start.27 = (f32[1,1,4,4,2,128]{5,4,3,2,1,0:T(2,128)S(1)}, f32[1,1,4,4,2,128]{5,4,3,2,1,0:T(2,128)S(1)}, u32[]{:S(2)}, u32[]{:S(2)}) collective-permute-start(f32[1,1,4,4,2,128]{5,4,3,2,1,0:T(2,128)S(1)} %slice.961), channel_id=1, source_target_pairs={{0,7},{1,0},{2,1},{3,2},{4,3},{5,4},{6,5},{7,6},{8,15},{9,8},{10,9... | collective-permute-start | bytes 49160 | tf_op jit(solution)/shard_map/ppermute | solution.py:120
  236.1 5.9 %collective-permute-start.29 = (f32[1,1,4,4,2,128]{5,4,3,2,1,0:T(2,128)S(1)}, f32[1,1,4,4,2,128]{5,4,3,2,1,0:T(2,128)S(1)}, u32[]{:S(2)}, u32[]{:S(2)}) collective-permute-start(f32[1,1,4,4,2,128]{5,4,3,2,1,0:T(2,128)S(1)} %slice.965), channel_id=1, source_target_pairs={{0,5},{1,6},{2,7},{3,0},{4,1},{5,2},{6,3},{7,4},{8,13},{9,14},{10,... | collective-permute-start | bytes 49160 | tf_op jit(solution)/shard_map/ppermute | solution.py:120
  244.2 9.1 %collective-permute-start.31 = (f32[1,1,4,4,2,128]{5,4,3,2,1,0:T(2,128)S(1)}, f32[1,1,4,4,2,128]{5,4,3,2,1,0:T(2,128)S(1)}, u32[]{:S(2)}, u32[]{:S(2)}) collective-permute-start(f32[1,1,4,4,2,128]{5,4,3,2,1,0:T(2,128)S(1)} %slice.969), channel_id=1, source_target_pairs={{0,3},{1,4},{2,5},{3,6},{4,7},{5,0},{6,1},{7,2},{8,11},{9,12},{10,... | collective-permute-start | bytes 49160 | tf_op jit(solution)/shard_map/ppermute | solution.py:120
  256.0 5.9 %collective-permute-start.33 = (f32[1,1,4,4,2,128]{5,4,3,2,1,0:T(2,128)S(1)}, f32[1,1,4,4,2,128]{5,4,3,2,1,0:T(2,128)S(1)}, u32[]{:S(2)}, u32[]{:S(2)}) collective-permute-start(f32[1,1,4,4,2,128]{5,4,3,2,1,0:T(2,128)S(1)} %slice.973), channel_id=1, source_target_pairs={{0,1},{1,2},{2,3},{3,4},{4,5},{5,6},{6,7},{7,0},{8,9},{9,10},{10,1... | collective-permute-start | bytes 49160 | tf_op jit(solution)/shard_map/ppermute | solution.py:120
  263.9 10.6 %collective-permute-start.35 = (f32[1,1,4,4,2,128]{5,4,3,2,1,0:T(2,128)S(1)}, f32[1,1,4,4,2,128]{5,4,3,2,1,0:T(2,128)S(1)}, u32[]{:S(2)}, u32[]{:S(2)}) collective-permute-start(f32[1,1,4,4,2,128]{5,4,3,2,1,0:T(2,128)S(1)} %slice.977), channel_id=1, source_target_pairs={{8,0},{16,8},{24,16},{32,24},{40,32},{48,40},{56,48},{64,56},{72,6... | collective-permute-start | bytes 49160 | tf_op jit(solution)/shard_map/ppermute | solution.py:26
  (253 shorter events, 97.5 us)
Async XLA Ops:
  3.9 39.7 %collective-permute-start = (f32[1,1,4,4,2,128]{5,4,3,2,1,0:T(2,128)S(1)}, f32[1,1,4,4,2,128]{5,4,3,2,1,0:T(2,128)S(1)}, u32[]{:S(2)}, u32[]{:S(2)}) collective-permute-start(f32[1,1,4,4,2,128]{5,4,3,2,1,0:T(2,128)S(1)} %maximum_bitcast_fusion), channel_id=1, source_target_pairs={{0,1},{1,2},{2,3},{3,4},{4,5},{5,6},{6,7},{7,0},{8,9},{9,10},{10,1... | collective-permute-start | bytes 49160 | tf_op jit(solution)/shard_map/ppermute | solution.py:120
  19.0 28.6 %collective-permute-start.1 = (f32[1,1,4,4,2,128]{5,4,3,2,1,0:T(2,128)S(1)}, f32[1,1,4,4,2,128]{5,4,3,2,1,0:T(2,128)S(1)}, u32[]{:S(2)}, u32[]{:S(2)}) collective-permute-start(f32[1,1,4,4,2,128]{5,4,3,2,1,0:T(2,128)S(1)} %maximum_bitcast_fusion), channel_id=1, source_target_pairs={{0,2},{1,3},{2,4},{3,5},{4,6},{5,7},{6,0},{7,1},{8,10},{9,11},{10,... | collective-permute-start | bytes 49160 | tf_op jit(solution)/shard_map/ppermute | solution.py:120
  22.4 29.7 %collective-permute-start.2 = (f32[1,1,4,4,2,128]{5,4,3,2,1,0:T(2,128)S(1)}, f32[1,1,4,4,2,128]{5,4,3,2,1,0:T(2,128)S(1)}, u32[]{:S(2)}, u32[]{:S(2)}) collective-permute-start(f32[1,1,4,4,2,128]{5,4,3,2,1,0:T(2,128)S(1)} %maximum_bitcast_fusion), channel_id=1, source_target_pairs={{0,3},{1,4},{2,5},{3,6},{4,7},{5,0},{6,1},{7,2},{8,11},{9,12},{10,... | collective-permute-start | bytes 49160 | tf_op jit(solution)/shard_map/ppermute | solution.py:120
  29.0 25.1 %collective-permute-start.3 = (f32[1,1,4,4,2,128]{5,4,3,2,1,0:T(2,128)S(1)}, f32[1,1,4,4,2,128]{5,4,3,2,1,0:T(2,128)S(1)}, u32[]{:S(2)}, u32[]{:S(2)}) collective-permute-start(f32[1,1,4,4,2,128]{5,4,3,2,1,0:T(2,128)S(1)} %maximum_bitcast_fusion), channel_id=1, source_target_pairs={{0,4},{1,5},{2,6},{3,7},{4,0},{5,1},{6,2},{7,3},{8,12},{9,13},{10,... | collective-permute-start | bytes 49160 | tf_op jit(solution)/shard_map/ppermute | solution.py:120
  30.9 33.8 %collective-permute-start.4 = (f32[1,1,4,4,2,128]{5,4,3,2,1,0:T(2,128)S(1)}, f32[1,1,4,4,2,128]{5,4,3,2,1,0:T(2,128)S(1)}, u32[]{:S(2)}, u32[]{:S(2)}) collective-permute-start(f32[1,1,4,4,2,128]{5,4,3,2,1,0:T(2,128)S(1)} %maximum_bitcast_fusion), channel_id=1, source_target_pairs={{0,5},{1,6},{2,7},{3,0},{4,1},{5,2},{6,3},{7,4},{8,13},{9,14},{10,... | collective-permute-start | bytes 49160 | tf_op jit(solution)/shard_map/ppermute | solution.py:120
  43.6 21.1 %collective-permute-start.5 = (f32[1,1,4,4,2,128]{5,4,3,2,1,0:T(2,128)S(1)}, f32[1,1,4,4,2,128]{5,4,3,2,1,0:T(2,128)S(1)}, u32[]{:S(2)}, u32[]{:S(2)}) collective-permute-start(f32[1,1,4,4,2,128]{5,4,3,2,1,0:T(2,128)S(1)} %maximum_bitcast_fusion), channel_id=1, source_target_pairs={{0,6},{1,7},{2,0},{3,1},{4,2},{5,3},{6,4},{7,5},{8,14},{9,15},{10,... | collective-permute-start | bytes 49160 | tf_op jit(solution)/shard_map/ppermute | solution.py:120
  79.3 30.6 %collective-permute-start.9 = (f32[1,1,4,4,2,128]{5,4,3,2,1,0:T(2,128)S(1)}, f32[1,1,4,4,2,128]{5,4,3,2,1,0:T(2,128)S(1)}, u32[]{:S(2)}, u32[]{:S(2)}) collective-permute-start(f32[1,1,4,4,2,128]{5,4,3,2,1,0:T(2,128)S(1)} %maximum_bitcast_fusion.1), channel_id=1, source_target_pairs={{0,1},{1,2},{2,3},{3,4},{4,5},{5,6},{6,7},{7,0},{8,9},{9,10},{10,1... | collective-permute-start | bytes 49160 | tf_op jit(solution)/shard_map/ppermute | solution.py:120
  87.6 24.8 %collective-permute-start.10 = (f32[1,1,4,4,2,128]{5,4,3,2,1,0:T(2,128)S(1)}, f32[1,1,4,4,2,128]{5,4,3,2,1,0:T(2,128)S(1)}, u32[]{:S(2)}, u32[]{:S(2)}) collective-permute-start(f32[1,1,4,4,2,128]{5,4,3,2,1,0:T(2,128)S(1)} %maximum_bitcast_fusion.1), channel_id=1, source_target_pairs={{0,2},{1,3},{2,4},{3,5},{4,6},{5,7},{6,0},{7,1},{8,10},{9,11},{10,... | collective-permute-start | bytes 49160 | tf_op jit(solution)/shard_map/ppermute | solution.py:120
  89.6 27.9 %collective-permute-start.11 = (f32[1,1,4,4,2,128]{5,4,3,2,1,0:T(2,128)S(1)}, f32[1,1,4,4,2,128]{5,4,3,2,1,0:T(2,128)S(1)}, u32[]{:S(2)}, u32[]{:S(2)}) collective-permute-start(f32[1,1,4,4,2,128]{5,4,3,2,1,0:T(2,128)S(1)} %maximum_bitcast_fusion.1), channel_id=1, source_target_pairs={{0,3},{1,4},{2,5},{3,6},{4,7},{5,0},{6,1},{7,2},{8,11},{9,12},{10,... | collective-permute-start | bytes 49160 | tf_op jit(solution)/shard_map/ppermute | solution.py:120
  95.5 24.5 %collective-permute-start.12 = (f32[1,1,4,4,2,128]{5,4,3,2,1,0:T(2,128)S(1)}, f32[1,1,4,4,2,128]{5,4,3,2,1,0:T(2,128)S(1)}, u32[]{:S(2)}, u32[]{:S(2)}) collective-permute-start(f32[1,1,4,4,2,128]{5,4,3,2,1,0:T(2,128)S(1)} %maximum_bitcast_fusion.1), channel_id=1, source_target_pairs={{0,4},{1,5},{2,6},{3,7},{4,0},{5,1},{6,2},{7,3},{8,12},{9,13},{10,... | collective-permute-start | bytes 49160 | tf_op jit(solution)/shard_map/ppermute | solution.py:120
  100.9 30.5 %collective-permute-start.13 = (f32[1,1,4,4,2,128]{5,4,3,2,1,0:T(2,128)S(1)}, f32[1,1,4,4,2,128]{5,4,3,2,1,0:T(2,128)S(1)}, u32[]{:S(2)}, u32[]{:S(2)}) collective-permute-start(f32[1,1,4,4,2,128]{5,4,3,2,1,0:T(2,128)S(1)} %maximum_bitcast_fusion.1), channel_id=1, source_target_pairs={{0,5},{1,6},{2,7},{3,0},{4,1},{5,2},{6,3},{7,4},{8,13},{9,14},{10,... | collective-permute-start | bytes 49160 | tf_op jit(solution)/shard_map/ppermute | solution.py:120
  109.9 22.1 %collective-permute-start.14 = (f32[1,1,4,4,2,128]{5,4,3,2,1,0:T(2,128)S(1)}, f32[1,1,4,4,2,128]{5,4,3,2,1,0:T(2,128)S(1)}, u32[]{:S(2)}, u32[]{:S(2)}) collective-permute-start(f32[1,1,4,4,2,128]{5,4,3,2,1,0:T(2,128)S(1)} %maximum_bitcast_fusion.1), channel_id=1, source_target_pairs={{0,6},{1,7},{2,0},{3,1},{4,2},{5,3},{6,4},{7,5},{8,14},{9,15},{10,... | collective-permute-start | bytes 49160 | tf_op jit(solution)/shard_map/ppermute | solution.py:120
  159.6 28.4 %collective-permute-start.18 = (f32[1,1,4,4,2,128]{5,4,3,2,1,0:T(2,128)S(1)}, f32[1,1,4,4,2,128]{5,4,3,2,1,0:T(2,128)S(1)}, u32[]{:S(2)}, u32[]{:S(2)}) collective-permute-start(f32[1,1,4,4,2,128]{5,4,3,2,1,0:T(2,128)S(1)} %slice.941), channel_id=1, source_target_pairs={{0,7},{1,0},{2,1},{3,2},{4,3},{5,4},{6,5},{7,6},{8,15},{9,8},{10,9... | collective-permute-start | bytes 49160 | tf_op jit(solution)/shard_map/ppermute | solution.py:120
  168.0 24.5 %collective-permute-start.19 = (f32[1,1,4,4,2,128]{5,4,3,2,1,0:T(2,128)S(1)}, f32[1,1,4,4,2,128]{5,4,3,2,1,0:T(2,128)S(1)}, u32[]{:S(2)}, u32[]{:S(2)}) collective-permute-start(f32[1,1,4,4,2,128]{5,4,3,2,1,0:T(2,128)S(1)} %slice.943), channel_id=1, source_target_pairs={{0,6},{1,7},{2,0},{3,1},{4,2},{5,3},{6,4},{7,5},{8,14},{9,15},{10,... | collective-permute-start | bytes 49160 | tf_op jit(solution)/shard_map/ppermute | solution.py:120
  171.3 25.7 %collective-permute-start.20 = (f32[1,1,4,4,2,128]{5,4,3,2,1,0:T(2,128)S(1)}, f32[1,1,4,4,2,128]{5,4,3,2,1,0:T(2,128)S(1)}, u32[]{:S(2)}, u32[]{:S(2)}) collective-permute-start(f32[1,1,4,4,2,128]{5,4,3,2,1,0:T(2,128)S(1)} %slice.945), channel_id=1, source_target_pairs={{0,5},{1,6},{2,7},{3,0},{4,1},{5,2},{6,3},{7,4},{8,13},{9,14},{10,... | collective-permute-start | bytes 49160 | tf_op jit(solution)/shard_map/ppermute | solution.py:120
  175.8 23.1 %collective-permute-start.21 = (f32[1,1,4,4,2,128]{5,4,3,2,1,0:T(2,128)S(1)}, f32[1,1,4,4,2,128]{5,4,3,2,1,0:T(2,128)S(1)}, u32[]{:S(2)}, u32[]{:S(2)}) collective-permute-start(f32[1,1,4,4,2,128]{5,4,3,2,1,0:T(2,128)S(1)} %slice.947), channel_id=1, source_target_pairs={{0,4},{1,5},{2,6},{3,7},{4,0},{5,1},{6,2},{7,3},{8,12},{9,13},{10,... | collective-permute-start | bytes 49160 | tf_op jit(solution)/shard_map/ppermute | solution.py:120
  181.3 28.6 %collective-permute-start.22 = (f32[1,1,4,4,2,128]{5,4,3,2,1,0:T(2,128)S(1)}, f32[1,1,4,4,2,128]{5,4,3,2,1,0:T(2,128)S(1)}, u32[]{:S(2)}, u32[]{:S(2)}) collective-permute-start(f32[1,1,4,4,2,128]{5,4,3,2,1,0:T(2,128)S(1)} %slice.949), channel_id=1, source_target_pairs={{0,3},{1,4},{2,5},{3,6},{4,7},{5,0},{6,1},{7,2},{8,11},{9,12},{10,... | collective-permute-start | bytes 49160 | tf_op jit(solution)/shard_map/ppermute | solution.py:120
  188.0 21.9 %collective-permute-start.23 = (f32[1,1,4,4,2,128]{5,4,3,2,1,0:T(2,128)S(1)}, f32[1,1,4,4,2,128]{5,4,3,2,1,0:T(2,128)S(1)}, u32[]{:S(2)}, u32[]{:S(2)}) collective-permute-start(f32[1,1,4,4,2,128]{5,4,3,2,1,0:T(2,128)S(1)} %slice.951), channel_id=1, source_target_pairs={{0,2},{1,3},{2,4},{3,5},{4,6},{5,7},{6,0},{7,1},{8,10},{9,11},{10,... | collective-permute-start | bytes 49160 | tf_op jit(solution)/shard_map/ppermute | solution.py:120
  224.9 28.6 %collective-permute-start.27 = (f32[1,1,4,4,2,128]{5,4,3,2,1,0:T(2,128)S(1)}, f32[1,1,4,4,2,128]{5,4,3,2,1,0:T(2,128)S(1)}, u32[]{:S(2)}, u32[]{:S(2)}) collective-permute-start(f32[1,1,4,4,2,128]{5,4,3,2,1,0:T(2,128)S(1)} %slice.961), channel_id=1, source_target_pairs={{0,7},{1,0},{2,1},{3,2},{4,3},{5,4},{6,5},{7,6},{8,15},{9,8},{10,9... | collective-permute-start | bytes 49160 | tf_op jit(solution)/shard_map/ppermute | solution.py:120
  233.5 22.5 %collective-permute-start.28 = (f32[1,1,4,4,2,128]{5,4,3,2,1,0:T(2,128)S(1)}, f32[1,1,4,4,2,128]{5,4,3,2,1,0:T(2,128)S(1)}, u32[]{:S(2)}, u32[]{:S(2)}) collective-permute-start(f32[1,1,4,4,2,128]{5,4,3,2,1,0:T(2,128)S(1)} %slice.963), channel_id=1, source_target_pairs={{0,6},{1,7},{2,0},{3,1},{4,2},{5,3},{6,4},{7,5},{8,14},{9,15},{10,... | collective-permute-start | bytes 49160 | tf_op jit(solution)/shard_map/ppermute | solution.py:120
  236.1 25.9 %collective-permute-start.29 = (f32[1,1,4,4,2,128]{5,4,3,2,1,0:T(2,128)S(1)}, f32[1,1,4,4,2,128]{5,4,3,2,1,0:T(2,128)S(1)}, u32[]{:S(2)}, u32[]{:S(2)}) collective-permute-start(f32[1,1,4,4,2,128]{5,4,3,2,1,0:T(2,128)S(1)} %slice.965), channel_id=1, source_target_pairs={{0,5},{1,6},{2,7},{3,0},{4,1},{5,2},{6,3},{7,4},{8,13},{9,14},{10,... | collective-permute-start | bytes 49160 | tf_op jit(solution)/shard_map/ppermute | solution.py:120
  242.0 21.9 %collective-permute-start.30 = (f32[1,1,4,4,2,128]{5,4,3,2,1,0:T(2,128)S(1)}, f32[1,1,4,4,2,128]{5,4,3,2,1,0:T(2,128)S(1)}, u32[]{:S(2)}, u32[]{:S(2)}) collective-permute-start(f32[1,1,4,4,2,128]{5,4,3,2,1,0:T(2,128)S(1)} %slice.967), channel_id=1, source_target_pairs={{0,4},{1,5},{2,6},{3,7},{4,0},{5,1},{6,2},{7,3},{8,12},{9,13},{10,... | collective-permute-start | bytes 49160 | tf_op jit(solution)/shard_map/ppermute | solution.py:120
  244.2 31.2 %collective-permute-start.31 = (f32[1,1,4,4,2,128]{5,4,3,2,1,0:T(2,128)S(1)}, f32[1,1,4,4,2,128]{5,4,3,2,1,0:T(2,128)S(1)}, u32[]{:S(2)}, u32[]{:S(2)}) collective-permute-start(f32[1,1,4,4,2,128]{5,4,3,2,1,0:T(2,128)S(1)} %slice.969), channel_id=1, source_target_pairs={{0,3},{1,4},{2,5},{3,6},{4,7},{5,0},{6,1},{7,2},{8,11},{9,12},{10,... | collective-permute-start | bytes 49160 | tf_op jit(solution)/shard_map/ppermute | solution.py:120
  253.5 22.0 %collective-permute-start.32 = (f32[1,1,4,4,2,128]{5,4,3,2,1,0:T(2,128)S(1)}, f32[1,1,4,4,2,128]{5,4,3,2,1,0:T(2,128)S(1)}, u32[]{:S(2)}, u32[]{:S(2)}) collective-permute-start(f32[1,1,4,4,2,128]{5,4,3,2,1,0:T(2,128)S(1)} %slice.971), channel_id=1, source_target_pairs={{0,2},{1,3},{2,4},{3,5},{4,6},{5,7},{6,0},{7,1},{8,10},{9,11},{10,... | collective-permute-start | bytes 49160 | tf_op jit(solution)/shard_map/ppermute | solution.py:120
  (31 other events, 403.4 us)
